TPU v7x, 32 devices: a whole 2x2x4 slice. The times are simulated.
32 devices in a mesh: dp: 8 (over z, x), mp: 4 (over y, core).
Axes of the slice: x: 2, y: 2, z: 4, core: 2. Of those that a mesh axis runs over, the one named last changes fastest.
Arguments:
- tokens: bfloat16 [64, 256, 768], P(('dp', 'mp')), may hold values from -6 to 6
- cotangent: bfloat16 [64, 256, 768], P(('dp', 'mp')), may hold values from -6 to 6
- segment_ids: int32 [64, 256], P('dp'), may hold values from 0 to 32, as said below
- live_mask: int32 [64, 256], P('dp'), may hold values from 0 to 1, as said below
- expert_ids: int32 [64], P('dp'), may hold values from 0 to 1, as said below
- qkv_weight: bfloat16 [768, 3, 768], P(None, None, 'mp'), may hold values from -0.21875 to 0.21875
- out_weight: bfloat16 [768, 768], P('mp'), may hold values from -0.875 to 0.875
- in_weight: bfloat16 [2, 768, 3072], P(None, None, 'mp'), may hold values from -0.21875 to 0.21875
- down_weight: bfloat16 [2, 3072, 768], P(None, 'mp'), may hold values from -0.15625 to 0.15625
- gain_attn: float32 [768], replicated, may hold values from 0.5 to 1.5
- shift_attn: float32 [768], replicated, may hold values from -3 to 3
- gain_ffn: float32 [768], replicated, may hold values from 0.5 to 1.5
- shift_ffn: float32 [768], replicated, may hold values from -3 to 3
Outputs:
- output: bfloat16 [64, 256, 768], P(('dp', 'mp'))
- grad_tokens: float32 [64, 256, 768], P(('dp', 'mp'))
- counts: int32 [2], replicated
- grad_qkv_weight: float32 [768, 3, 768], P(None, None, 'mp')
- grad_out_weight: float32 [768, 768], P('mp')
- grad_in_weight: float32 [2, 768, 3072], P(None, None, 'mp')
- grad_down_weight: float32 [2, 3072, 768], P(None, 'mp')
- grad_gain_attn: float32 [768], replicated
- grad_shift_attn: float32 [768], replicated
- grad_gain_ffn: float32 [768], replicated
- grad_shift_ffn: float32 [768], replicated
Inputs may be any that keep to these rules, and one draw needn't show every extreme that they name: `segment_ids`: ids never fall along a row; the live slots with one id form one caption of 8 to 40 tokens, and captions of both lengths occur; padding slots carry the id 32. `live_mask`: each row is 1 on its first live slots and 0 on the padding after them; every row has live slots. `expert_ids`: every expert is named by some row.
All inputs are finite; a program needn't handle non-finite values.
Results may differ from a plain program's by a relative error of at most 0.018.
Values may be sent and summed in bfloat16 or wider, within the bound.
No kernel may reach another device: no remote copies, remote signals or barrier semaphores. Data moves between devices by JAX's collectives and lax.ppermute only.
A program may use at most 128 MiB of HBM per device.

v0:
```python
import jax
import jax.numpy as jnp
from jax import lax
from jax.sharding import PartitionSpec as P

HD = 64
norm_epsilon = 1e-05
masked_fill = -1e30


def layer_norm(values, norm_gain, norm_shift):
    average = jnp.mean(values, axis=-1, keepdims=True)
    centred = values - average
    variance = jnp.mean(centred * centred, axis=-1, keepdims=True)
    return centred * lax.rsqrt(variance + norm_epsilon) * norm_gain + norm_shift


def gelu_exact(values):
    return jax.nn.gelu(values, approximate=False)


def select_rows(values, hot_column):
    return values * hot_column[:, None, None]


def per_device(
    tokens,
    cotangent,
    segment_ids,
    live_mask,
    expert_ids,
    qkv_weight,
    out_weight,
    in_weight,
    down_weight,
    gain_attn,
    shift_attn,
    gain_ffn,
    shift_ffn,
):
    local_rows, slots, model_width = tokens.shape
    experts = in_weight.shape[0]
    heads_local = qkv_weight.shape[2] // HD
    score_scale = HD ** (-0.5)
    first_row = lax.axis_index("mp") * local_rows
    expert_hot = expert_ids[:, None] == jnp.arange(experts)[None, :]
    row_live = jnp.sum(live_mask, axis=1)
    local_counts = jnp.sum(jnp.where(expert_hot, row_live[:, None], 0), axis=0)
    counts = lax.psum(local_counts, "dp")
    hot_matrix = expert_hot.astype(jnp.bfloat16)
    token_float = tokens.astype(jnp.float32)
    norm_one = layer_norm(token_float, gain_attn, shift_attn).astype(jnp.bfloat16)
    norm_one_full = lax.all_gather(norm_one, "mp", axis=0, tiled=True)
    qkv_flat = qkv_weight.reshape(model_width, -1)
    qkv_all = jnp.einsum(
        "rsd,dk->rsk", norm_one_full, qkv_flat, preferred_element_type=jnp.float32
    ).astype(jnp.bfloat16)
    group_rows = qkv_all.shape[0]
    qkv_split = qkv_all.reshape(group_rows, slots, 3, heads_local, HD)
    queries = qkv_split[:, :, 0]
    key_part = qkv_split[:, :, 1]
    value_part = qkv_split[:, :, 2]
    same_caption = segment_ids[:, :, None] == segment_ids[:, None, :]
    diagonal = jnp.arange(slots)[:, None] == jnp.arange(slots)[None, :]
    allowed = (same_caption & ((live_mask[:, None, :] == 1) | diagonal[None]))[:, None]

    def masked_scores():
        raw_scores = (
            jnp.einsum("rqhd,rkhd->rhqk", queries, key_part, preferred_element_type=jnp.float32)
            * score_scale
        )
        return jnp.where(allowed, raw_scores, masked_fill)

    scores = masked_scores()
    row_top = jnp.max(scores, axis=-1, keepdims=True)
    exp_scores = jnp.exp(scores - row_top)
    row_total = jnp.sum(exp_scores, axis=-1, keepdims=True)
    attn_probs = exp_scores / row_total
    log_total = row_top + jnp.log(row_total)
    head_mix = jnp.einsum(
        "rhqk,rkhd->rqhd",
        attn_probs.astype(jnp.bfloat16),
        value_part,
        preferred_element_type=jnp.float32,
    )
    head_mix = head_mix.reshape(group_rows, slots, heads_local * HD).astype(jnp.bfloat16)
    picked = head_mix
    attn_local = lax.psum_scatter(
        jnp.einsum("rsk,kd->rsd", picked, out_weight, preferred_element_type=jnp.float32).astype(
            jnp.bfloat16
        ),
        "mp",
        scatter_dimension=0,
        tiled=True,
    ).astype(jnp.float32)
    residual = token_float + attn_local
    norm_two = layer_norm(residual, gain_ffn, shift_ffn).astype(jnp.bfloat16)
    norm_two_full = lax.all_gather(norm_two, "mp", axis=0, tiled=True)
    upward = jnp.zeros((group_rows, slots, in_weight.shape[2]), jnp.float32)
    for expert in range(experts):
        upward = upward + jnp.einsum(
            "rsd,df->rsf",
            select_rows(norm_two_full, hot_matrix[:, expert]),
            in_weight[expert],
            preferred_element_type=jnp.float32,
        )
    activated = gelu_exact(upward).astype(jnp.bfloat16)
    picked = activated
    hot_picked = hot_matrix
    total = jnp.zeros((local_rows * lax.axis_size("mp"), slots, model_width), jnp.float32)
    for ffn_expert in range(experts):
        total = total + jnp.einsum(
            "rsf,fd->rsd",
            select_rows(picked, hot_picked[:, ffn_expert]),
            down_weight[ffn_expert],
            preferred_element_type=jnp.float32,
        )
    ffn_local = lax.psum_scatter(
        total.astype(jnp.bfloat16), "mp", scatter_dimension=0, tiled=True
    ).astype(jnp.float32)
    output = (residual + ffn_local).astype(jnp.bfloat16)
    count_float = counts.astype(jnp.float32)
    loss_weight = jnp.sum(count_float) / (experts * count_float)
    local_hot = lax.dynamic_slice_in_dim(expert_hot, first_row, local_rows, 0)
    row_weight = jnp.sum(jnp.where(local_hot, loss_weight[None, :], 0.0), axis=1)
    live_local = lax.dynamic_slice_in_dim(live_mask, first_row, local_rows, 0)
    grad_output = (
        cotangent.astype(jnp.float32)
        * live_local[:, :, None].astype(jnp.float32)
        * row_weight[:, None, None]
    )
    grad_ffn_full = lax.all_gather(grad_output.astype(jnp.bfloat16), "mp", axis=0, tiled=True)
    grad_act = jnp.zeros(upward.shape, jnp.float32)
    down_list = []
    for expert in range(experts):
        masked_grad = select_rows(grad_ffn_full, hot_matrix[:, expert])
        grad_act = grad_act + jnp.einsum(
            "rsd,fd->rsf", masked_grad, down_weight[expert], preferred_element_type=jnp.float32
        )
        down_list.append(
            jnp.einsum("rsf,rsd->fd", activated, masked_grad, preferred_element_type=jnp.float32)
        )
    grad_down_weight = jnp.stack(down_list, axis=0)
    grad_up = jax.vjp(gelu_exact, upward)[1](grad_act)[0].astype(jnp.bfloat16)
    in_list = []
    for expert in range(experts):
        in_list.append(
            jnp.einsum(
                "rsd,rsf->df",
                select_rows(norm_two_full, hot_matrix[:, expert]),
                grad_up,
                preferred_element_type=jnp.float32,
            )
        )
    grad_in_weight = jnp.stack(in_list, axis=0)
    picked = grad_up
    hot_picked = hot_matrix
    total = jnp.zeros((local_rows * lax.axis_size("mp"), slots, model_width), jnp.float32)
    for expert in range(experts):
        total = total + jnp.einsum(
            "rsf,df->rsd",
            select_rows(picked, hot_picked[:, expert]),
            in_weight[expert],
            preferred_element_type=jnp.float32,
        )
    grad_norm_two = lax.psum_scatter(
        total.astype(jnp.bfloat16), "mp", scatter_dimension=0, tiled=True
    ).astype(jnp.float32)
    second_back = jax.vjp(layer_norm, residual, gain_ffn, shift_ffn)[1]
    grad_from_second, grad_gain_ffn, grad_shift_ffn = second_back(grad_norm_two)
    grad_residual = grad_output + grad_from_second
    grad_attn_full = lax.all_gather(grad_residual.astype(jnp.bfloat16), "mp", axis=0, tiled=True)
    grad_out_weight = jnp.einsum(
        "rsk,rsd->kd", head_mix, grad_attn_full, preferred_element_type=jnp.float32
    )
    grad_mix = jnp.einsum(
        "rsd,kd->rsk", grad_attn_full, out_weight, preferred_element_type=jnp.float32
    )
    grad_mix = grad_mix.astype(jnp.bfloat16).reshape(group_rows, slots, heads_local, HD)
    attn_again = jnp.exp(masked_scores() - log_total)
    grad_probs = jnp.einsum(
        "rqhd,rkhd->rhqk", grad_mix, value_part, preferred_element_type=jnp.float32
    )
    grad_scores = attn_again * (
        grad_probs - jnp.sum(grad_probs * attn_again, axis=-1, keepdims=True)
    )
    grad_scores = grad_scores.astype(jnp.bfloat16)
    grad_value = jnp.einsum(
        "rhqk,rqhd->rkhd",
        attn_again.astype(jnp.bfloat16),
        grad_mix,
        preferred_element_type=jnp.float32,
    )
    grad_query = (
        jnp.einsum("rhqk,rkhd->rqhd", grad_scores, key_part, preferred_element_type=jnp.float32)
        * score_scale
    )
    grad_key = (
        jnp.einsum("rhqk,rqhd->rkhd", grad_scores, queries, preferred_element_type=jnp.float32)
        * score_scale
    )
    grad_qkv = (
        jnp.stack([grad_query, grad_key, grad_value], axis=2)
        .astype(jnp.bfloat16)
        .reshape(group_rows, slots, -1)
    )
    grad_qkv_weight = jnp.einsum(
        "rsd,rsk->dk", norm_one_full, grad_qkv, preferred_element_type=jnp.float32
    )
    grad_qkv_weight = grad_qkv_weight.reshape(qkv_weight.shape)
    picked = grad_qkv
    grad_norm_one = lax.psum_scatter(
        jnp.einsum("rsk,dk->rsd", picked, qkv_flat, preferred_element_type=jnp.float32).astype(
            jnp.bfloat16
        ),
        "mp",
        scatter_dimension=0,
        tiled=True,
    ).astype(jnp.float32)
    first_back = jax.vjp(layer_norm, token_float, gain_attn, shift_attn)[1]
    grad_from_first, grad_gain_attn, grad_shift_attn = first_back(grad_norm_one)
    grad_tokens = grad_residual + grad_from_first
    norm_grads = lax.psum(
        (grad_gain_attn, grad_shift_attn, grad_gain_ffn, grad_shift_ffn), ("dp", "mp")
    )
    summed = lax.psum((grad_qkv_weight, grad_out_weight, grad_in_weight, grad_down_weight), "dp")
    return (
        output,
        grad_tokens,
        counts,
        summed[0],
        summed[1],
        summed[2],
        summed[3],
        norm_grads[0],
        norm_grads[1],
        norm_grads[2],
        norm_grads[3],
    )


def solution(mesh):
    in_specs = (
        P(("dp", "mp"), None, None),
        P(("dp", "mp"), None, None),
        P("dp", None),
        P("dp", None),
        P("dp"),
        P(None, None, "mp"),
        P("mp", None),
        P(None, None, "mp"),
        P(None, "mp", None),
        P(),
        P(),
        P(),
        P(),
    )
    out_specs = (
        P(("dp", "mp"), None, None),
        P(("dp", "mp"), None, None),
        P(),
        P(None, None, "mp"),
        P("mp", None),
        P(None, None, "mp"),
        P(None, "mp", None),
        P(),
        P(),
        P(),
        P(),
    )
    return jax.shard_map(
        per_device, mesh=mesh, in_specs=in_specs, out_specs=out_specs, check_vma=False
    )
```

profile of v0, /device:TPU:0, one launch (start us, length us, event | category | flops | bytes accessed | tf_op | source)
XLA Modules:
  0.0 761.4 jit_solution(12436911673130633448)
XLA Ops:
  7.3 1.4 convert_reduce_fusion.2
  8.6 1.5 fusion.70
  10.2 2.4 fusion.68
  12.7 0.7 or_and_fusion
  13.4 30.5 %all-gather.5.cloned.1.call-done = bf16[8,256,768]{2,1,0:T(8,128)(2,1)} async-done(((bf16[2,256,768]{2,1,0:T(8,128)(2,1)}), bf16[8,256,768]{2,1,0:T(8,128)(2,1)}) %all-gather.5.cloned.1.call-update) | async-done | bytes 3145744 | tf_op jit(solution)/shard_map/all_gather | solution.py:53
  44.0 3.9 convolution_convert_fusion.2
  47.9 1.3 fusion.125
  49.3 1.1 fusion.6
  50.4 1.5 copy-done.2
  51.9 1.2 fusion.95
  53.1 0.9 copy-done.10
  54.0 2.7 convolution_convert_fusion.1
  57.1 11.4 %psum.63 = s32[2]{0:T(128)S(1)} all-reduce(s32[2]{0:T(128)S(1)} %select_reduce_fusion), channel_id=1, replica_groups=mesh['dp'=8,'mp'=4] {'dp'}, use_global_device_ids=true, to_apply=%region_10.11 | all-reduce | flops 2 | bytes 16 | tf_op jit(solution)/shard_map/psum | solution.py:49
  68.4 0.6 convert_reduce_fusion.3
  69.0 0.7 multiply_divide_fusion
  69.8 1.1 fusion.74
  71.0 23.8 %reduce-scatter.5.cloned.1.call-done = bf16[2,256,768]{2,1,0:T(8,128)(2,1)} async-done(((bf16[8,256,768]{2,1,0:T(8,128)(2,1)}), bf16[2,256,768]{2,1,0:T(8,128)(2,1)}) %reduce-scatter.5.cloned.1.call-update) | async-done | bytes 786448 | tf_op jit(solution)/shard_map/reduce_scatter | solution.py:88
  94.8 1.5 fusion.97
  96.3 1.5 multiply_reduce_fusion.1
  97.9 1.3 add_convert_fusion.4
  99.5 26.0 %all-gather.9.cloned.1.call-done = bf16[8,256,768]{2,1,0:T(8,128)(2,1)} async-done(((bf16[2,256,768]{2,1,0:T(8,128)(2,1)}), bf16[8,256,768]{2,1,0:T(8,128)(2,1)}) %all-gather.9.cloned.1.call-update) | async-done | bytes 3145744 | tf_op jit(solution)/shard_map/all_gather | solution.py:132
  125.5 7.5 fusion.24
  133.0 23.0 %all-gather.7.cloned.1.call-done = bf16[8,256,768]{2,1,0:T(8,128)(2,1)} async-done(((bf16[2,256,768]{2,1,0:T(8,128)(2,1)}), bf16[8,256,768]{2,1,0:T(8,128)(2,1)}) %all-gather.7.cloned.1.call-update) | async-done | bytes 3145744 | tf_op jit(solution)/shard_map/all_gather | solution.py:98
  156.0 5.1 fusion.32
  161.1 4.6 fusion.88
  165.7 15.1 %multiply_convert_fusion.1 = (bf16[8,256,768]{2,1,0:T(8,128)(2,1)}, f32[8,256,768]{2,1,0:T(8,128)S(1)}) fusion(f32[8,256,768]{2,1,0:T(8,128)S(1)} %get-tuple-element.39, u8[256,768]{1,0:T(8,128)(4,1)S(1)} %get-tuple-element.12, u8[256,768]{1,0:T(8,128)(4,1)S(1)} %get-tuple-element.11), kind=kLoop, calls=%fused_computation.13 | loop fusion | flops 110100480 | bytes 16121856 | tf_op jit(solution)/shard_map/convert_element_type | solution.py:107
  180.8 10.6 %add_convert_fusion.1 = bf16[8,256,768]{2,1,0:T(8,128)(2,1)} fusion(f32[8,256,768]{2,1,0:T(8,128)S(1)} %get-tuple-element.30, f32[8,256,768]{2,1,0:T(8,128)} %fusion.24, f32[8,256,768]{2,1,0:T(8,128)S(1)} %get-tuple-element.39, bf16[8,256,768]{2,1,0:T(8,128)(2,1)} %all-gather.9.cloned.1.call-done, bf16[8]{0:T(256)(128)(2,1)S(1)} %get-tuple-element.35, ...), kind=kOutput, calls=%fused_computation.11 | convolution fusion | flops 2441084928 | bytes 26345488 | tf_op jit(solution)/shard_map/rsd,fd->rsf/dot_general | solution.py:137
  191.4 4.7 fusion.13
  196.2 4.1 add_convert_fusion
  200.3 38.0 %reduce-scatter.9.cloned.1.call-done = bf16[2,256,768]{2,1,0:T(8,128)(2,1)} async-done(((bf16[8,256,768]{2,1,0:T(8,128)(2,1)}), bf16[2,256,768]{2,1,0:T(8,128)(2,1)}) %reduce-scatter.9.cloned.1.call-update) | async-done | bytes 786448 | tf_op jit(solution)/shard_map/reduce_scatter | solution.py:166
  238.3 1.9 convert_reduce_fusion.1
  240.2 2.2 fusion.72
  242.4 2.8 fusion.115
  245.5 28.4 %all-gather.11.cloned.1.call-done = bf16[8,256,768]{2,1,0:T(8,128)(2,1)} async-done(((bf16[2,256,768]{2,1,0:T(8,128)(2,1)}), bf16[8,256,768]{2,1,0:T(8,128)(2,1)}) %all-gather.11.cloned.1.call-update) | async-done | bytes 3145744 | tf_op jit(solution)/shard_map/all_gather | solution.py:172
  273.9 3.2 convolution_convert_fusion.3
  277.2 4.0 fusion.92
  281.2 5.3 multiply_reduce_fusion
  286.5 4.6 multiply_convert_fusion
  291.1 1.1 multiply_bitcast_fusion
  292.2 0.7 multiply_bitcast_fusion.1
  292.9 0.3 maximum_convert_fusion
  293.1 1.4 copy-done.5
  294.6 0.3 copy.69
  294.9 4.1 convolution_convert_fusion
  299.0 5.1 fusion.17
  304.1 4.1 add_convert_fusion.2
  308.5 5.9 fusion.58
  314.5 2.8 fusion.55
  317.3 0.4 copy-done.22
  317.7 2.8 fusion.64
  320.5 2.8 fusion.61
  323.3 4.4 pad_maximum_fusion
  327.7 1.6 convolution_bitcast_fusion
  329.4 5.4 fusion.89
  334.8 2.2 reduce-scatter.11.cloned.1.call-done
  337.0 1.7 convert_reduce_fusion
  338.7 2.1 fusion.73
  340.8 39.9 %all-reduce = (f32[768]{0:T(1024)}, f32[768]{0:T(1024)}, f32[768]{0:T(1024)}, f32[768]{0:T(1024)}) all-reduce(f32[768]{0:T(1024)S(1)} %get-tuple-element.15, f32[768]{0:T(1024)S(1)} %get-tuple-element.19, f32[768]{0:T(1024)S(1)} %get-tuple-element.13, f32[768]{0:T(1024)S(1)} %get-tuple-element.17), channel_id=1, replica_groups=mesh['dp'=8,'mp'=4] {'dp','mp'}, use_global_device_ids=true, to_apply=%region_25.26 | all-reduce | flops 3072 | bytes 24576 | tf_op jit(solution)/shard_map/psum | solution.py:223
  380.7 3.7 add_add_fusion.2
  384.4 360.6 %all-reduce.4.cloned.1.call-done = (f32[768,3,192]{0,2,1:T(8,128)}, f32[192,768]{1,0:T(8,128)}, f32[2,768,768]{2,1,0:T(8,128)}, f32[2,768,768]{2,1,0:T(8,128)}) async-done(((f32[768,3,192]{0,2,1:T(8,128)}, f32[192,768]{1,0:T(8,128)}, f32[2,768,768]{2,1,0:T(8,128)}, f32[2,768,768]{2,1,0:T(8,128)}), (f32[768,3,192]{0,2,1:T(8,128)}, f32[192,768]{1,0:T(8,128)}, f32[2,768,768]{2,1,0:T(8,128)}, ...) | async-done | bytes 11796496 | tf_op jit(solution)/shard_map/psum | solution.py:226
  745.0 2.9 copy.95
  748.0 2.1 copy.96
  750.0 2.2 copy.97
  752.2 2.2 copy.98
  (104 shorter events, 1.8 us)
Async XLA Ops:
  7.2 36.8 %copy-start = (bf16[768,3,192]{0,2,1:T(8,128)(2,1)S(1)}, bf16[768,3,192]{0,2,1:T(8,128)(2,1)}, u32[]{:S(2)}) copy-start(bf16[768,3,192]{0,2,1:T(8,128)(2,1)} %param.18) | copy-start | bytes 2654212
  7.2 5.5 copy-start.19
  7.2 5.5 copy-start.20
  7.2 36.8 %all-gather.5.cloned.1.call-start = ((), (), s32[]{:S(2)}) async-start(), calls=%async_computation.4 | async-start | bytes 3932160 | tf_op jit(solution)/shard_map/all_gather | solution.py:53
  12.6 82.2 %reduce-scatter.5.cloned.1.call-start = ((), (), s32[]{:S(2)}) async-start(), calls=%async_computation.5 | async-start | bytes 3932160 | tf_op jit(solution)/shard_map/reduce_scatter | solution.py:88
  47.9 2.5 copy-start.14
  49.2 2.7 copy-start.2
  51.9 2.1 copy-start.16
  53.1 0.9 copy-start.10
  54.0 2.9 copy-start.27
  54.0 15.8 %copy-start.7 = (bf16[2,256,768]{2,1,0:T(8,128)(2,1)S(1)}, bf16[2,256,768]{2,1,0:T(8,128)(2,1)}, u32[]{:S(2)}) copy-start(bf16[2,256,768]{2,1,0:T(8,128)(2,1)} %param.14) | copy-start | bytes 2359300
  56.7 38.1 %copy-start.1 = (bf16[2,256,768]{2,1,0:T(8,128)(2,1)S(1)}, bf16[2,256,768]{2,1,0:T(8,128)(2,1)}, u32[]{:S(2)}) copy-start(bf16[2,256,768]{2,1,0:T(8,128)(2,1)} %param.13) | copy-start | bytes 2359300
  56.8 41.1 %copy-start.17 = (f32[768]{0:T(1024)S(1)}, f32[768]{0:T(1024)}, u32[]{:S(2)}) copy-start(f32[768]{0:T(1024)} %param.24) | copy-start | bytes 9220
  56.8 41.1 %copy-start.21 = (f32[768]{0:T(1024)S(1)}, f32[768]{0:T(1024)}, u32[]{:S(2)}) copy-start(f32[768]{0:T(1024)} %param.25) | copy-start | bytes 9220
  56.8 68.7 %all-gather.9.cloned.1.call-start = ((), (), s32[]{:S(2)}) async-start(), calls=%async_computation.8 | async-start | bytes 3932160 | tf_op jit(solution)/shard_map/all_gather | solution.py:132
  68.4 30.7 %copy-start.28 = (s32[2]{0:T(128)}, s32[2]{0:T(128)S(1)}, u32[]{:S(2)}) copy-start(s32[2]{0:T(128)S(1)} %psum.63) | copy-start | bytes 28
  71.0 85.0 %all-gather.7.cloned.1.call-start = ((), (), s32[]{:S(2)}) async-start(), calls=%async_computation.6 | async-start | bytes 3932160 | tf_op jit(solution)/shard_map/all_gather | solution.py:98
  94.8 3.1 copy-start.3
  99.2 139.1 %reduce-scatter.9.cloned.1.call-start = ((), (), s32[]{:S(2)}) async-start(), calls=%async_computation.9 | async-start | bytes 3932160 | tf_op jit(solution)/shard_map/reduce_scatter | solution.py:166
  156.0 5.1 copy-start.23
  156.0 5.1 copy-start.25
  191.4 4.7 copy-start.29
  200.3 73.6 %all-gather.11.cloned.1.call-start = ((), (), s32[]{:S(2)}) async-start(), calls=%async_computation.10 | async-start | bytes 3932160 | tf_op jit(solution)/shard_map/all_gather | solution.py:172
  238.3 4.1 copy-start.4
  245.3 91.8 %reduce-scatter.11.cloned.1.call-start = ((), (), s32[]{:S(2)}) async-start(), calls=%async_computation.11 | async-start | bytes 3932160 | tf_op jit(solution)/shard_map/reduce_scatter | solution.py:212
  273.9 7.3 slice-start
  277.2 4.1 slice-start.1
  286.5 4.6 copy-start.15
  293.1 1.5 copy-start.5
  299.0 81.7 %reduce-scatter.7.cloned.1.call-start = ((), (), s32[]{:S(2)}) async-start(), calls=%async_computation.7 | async-start | bytes 3932160 | tf_op jit(solution)/shard_map/reduce_scatter | solution.py:118
  299.0 5.1 copy-start.12
  299.0 5.1 copy-start.26
  308.2 436.8 %all-reduce.4.cloned.1.call-start = ((), (), s32[]{:S(2)}) async-start(), calls=%async_computation.12 | async-start | bytes 23592960 | tf_op jit(solution)/shard_map/psum | solution.py:226
  308.5 5.9 copy-start.24
  308.5 5.9 copy-start.30
  314.4 2.9 copy-start.13
  314.4 3.2 copy-start.22
  323.3 4.4 copy-start.9
  323.3 4.4 copy-start.11
  327.7 1.7 copy-start.6
  334.8 2.2 copy-start.18
  745.0 5.0 copy-start.8
  748.0 4.3 slice-start.2
  750.0 2.2 slice-start.3
Sparse Core Ops, SparseCore 0:
  12.7 31.2 all-gather.4
  56.9 37.8 reduce-scatter.4
  96.9 28.4 all-gather.8
  127.5 28.4 all-gather.6
  200.4 37.8 reduce-scatter.8
  245.4 28.5 all-gather.10
  299.1 37.8 reduce-scatter.10
  339.5 38.0 reduce-scatter.6
  382.8 362.1 all-reduce.3
where the time goes:
time: 769 us; the launch traced here: 761 us
  waiting for transfers between devices  533 us (69%)
  matrix products  94.5 us (12%)
  other arithmetic  52.9 us (7%)
  blocking collectives  51.2 us (7%)
  between operations  14.8 us (2%)
  local copies, waits for them, and re-layouts  14.1 us (2%)
    psum x1, waiting for transfers between devices, per_device(): lax.psum((grad_qkv_weight, grad_out_weight, grad_in_weight, grad_down_wei...  361 us
    psum x1, blocking collectives, per_device(): lax.psum((grad_gain_attn, grad_shift_attn, grad_gain_ffn, grad_shift_ffn)...  39.9 us
    reduce_scatter x2, waiting for transfers between devices, per_device(): lax.psum_scatter(total.astype(jnp.bfloat16), 'mp', scatter_dimension=0, t...  38 us
    all_gather x1, waiting for transfers between devices, per_device(): norm_one_full = lax.all_gather(norm_one, 'mp', axis=0, tiled=True)  30.5 us
    all_gather x1, waiting for transfers between devices, per_device(): lax.all_gather(grad_residual.astype(jnp.bfloat16), 'mp', axis=0, tiled=True)  28.4 us
    all_gather x1, waiting for transfers between devices, per_device(): lax.all_gather(grad_output.astype(jnp.bfloat16), 'mp', axis=0, tiled=True)  26 us
    reduce_scatter x1, waiting for transfers between devices, per_device(): lax.psum_scatter(jnp.einsum('rsk,kd->rsd', picked, out_weight, preferred_...  23.8 us
    all_gather x1, waiting for transfers between devices, per_device(): norm_two_full = lax.all_gather(norm_two, 'mp', axis=0, tiled=True)  23 us
  transfers between devices with their start and end apart: 9, of which 8 were waited for; matrix products, arithmetic and copies ran while one was open for 8% of the time, Pallas kernels for 0%

commit v1 on v0

--- a/solution.py
+++ b/solution.py
@@ -6,6 +6,12 @@
 HD = 64
 norm_epsilon = 1e-05
 masked_fill = -1e30
+
+
+def joined_along(blocks, dim):
+    blocks = jnp.moveaxis(blocks, 0, dim)
+    shape = blocks.shape
+    return blocks.reshape(*shape[:dim], shape[dim] * shape[dim + 1], *shape[dim + 2 :])
 
 
 def layer_norm(values, norm_gain, norm_shift):
@@ -129,7 +135,20 @@
         * live_local[:, :, None].astype(jnp.float32)
         * row_weight[:, None, None]
     )
-    grad_ffn_full = lax.all_gather(grad_output.astype(jnp.bfloat16), "mp", axis=0, tiled=True)
+    array = grad_output.astype(jnp.bfloat16)
+    size = lax.axis_size("mp")
+    pairs = [(i, (i + 1) % size) for i in range(size)]
+    back = [(b, a) for a, b in pairs]
+    lower, upper = ([], [])
+    for step in range(size - 1):
+        if step % 2 == 0:
+            lower.append(lax.ppermute(lower[-1] if lower else array, "mp", pairs))
+        else:
+            upper.append(lax.ppermute(upper[-1] if upper else array, "mp", back))
+    pieces = jnp.stack([*lower[::-1], array, *upper])
+    shift = lax.axis_index("mp") - len(lower)
+    pieces = pieces[(jnp.arange(size) - shift) % size]
+    grad_ffn_full = joined_along(pieces, 0)
     grad_act = jnp.zeros(upward.shape, jnp.float32)
     down_list = []
     for expert in range(experts):

time: 769 us -> 778 us (1.012)
  matrix products: 94.5 us -> 83.3 us
  other arithmetic: 52.9 us -> 62.5 us
    ppermute x0 -> x3, waiting for transfers between devices: none -> 39.2 us  [the longest x2 39.2 us: per_device(): lower.append(lax.ppermute(lower[-1] if lower else array, 'mp', pairs))]
    all_gather x1 -> x0, waiting for transfers between devices: 26 us -> none  [per_device(): lax.all_gather(grad_output.astype(jnp.bfloat16), 'mp', axis=0, tiled=True)]
    all_gather x1, waiting for transfers between devices: 23 us -> 0.01 us  [per_device(): norm_two_full = lax.all_gather(norm_two, 'mp', axis=0, tiled=True)]
    reduce_scatter x1, waiting for transfers between devices: 23.8 us -> 38 us  [per_device(): lax.psum_scatter(jnp.einsum('rsk,kd->rsd', picked, out_weight, preferred_...]
    unnamed x74 -> x80, local copies, waits for them, and re-layouts: 13.9 us -> 16.1 us
  transfers between devices with their start and end apart: 9 -> 11, of which waited for: 8 -> 8; matrix products, arithmetic and copies ran while one was open for 8% -> 8% of each run, Pallas kernels for 0% -> 0%
where the time goes in v1:
time: 778 us; the launch traced here: 771 us
  waiting for transfers between devices  535 us (69%)
  matrix products  83.3 us (11%)
  other arithmetic  62.5 us (8%)
  blocking collectives  51.7 us (7%)
  local copies, waits for them, and re-layouts  20.9 us (3%)
  between operations  15.1 us (2%)
    psum x1, waiting for transfers between devices, per_device(): lax.psum((grad_qkv_weight, grad_out_weight, grad_in_weight, grad_down_wei...  360 us
    psum x1, blocking collectives, per_device(): lax.psum((grad_gain_attn, grad_shift_attn, grad_gain_ffn, grad_shift_ffn)...  40.3 us
    ppermute x2, waiting for transfers between devices, per_device(): lower.append(lax.ppermute(lower[-1] if lower else array, 'mp', pairs))  39.2 us
    reduce_scatter x2, waiting for transfers between devices, per_device(): lax.psum_scatter(total.astype(jnp.bfloat16), 'mp', scatter_dimension=0, t...  38 us
    reduce_scatter x1, waiting for transfers between devices, per_device(): lax.psum_scatter(jnp.einsum('rsk,kd->rsd', picked, out_weight, preferred_...  38 us
    all_gather x1, waiting for transfers between devices, per_device(): norm_one_full = lax.all_gather(norm_one, 'mp', axis=0, tiled=True)  30.5 us
    all_gather x1, waiting for transfers between devices, per_device(): lax.all_gather(grad_residual.astype(jnp.bfloat16), 'mp', axis=0, tiled=True)  28.4 us
    unnamed x80, local copies, waits for them, and re-layouts  16.1 us
  transfers between devices with their start and end apart: 11, of which 8 were waited for; matrix products, arithmetic and copies ran while one was open for 8% of the time, Pallas kernels for 0%

profile of v1, /device:TPU:0, one launch (start us, length us, event | category | flops | bytes accessed | tf_op | source)
XLA Modules:
  0.0 770.9 jit_solution(15547384919574644097)
XLA Ops:
  7.3 1.4 convert_reduce_fusion.2
  8.6 1.5 fusion.54
  10.2 2.4 fusion.52
  12.7 0.7 or_and_fusion
  13.4 30.5 %all-gather.4.cloned.1.call-done = bf16[8,256,768]{2,1,0:T(8,128)(2,1)} async-done(((bf16[2,256,768]{2,1,0:T(8,128)(2,1)}), bf16[8,256,768]{2,1,0:T(8,128)(2,1)}) %all-gather.4.cloned.1.call-update) | async-done | bytes 3145744 | tf_op jit(solution)/shard_map/all_gather | solution.py:59
  44.0 3.9 convolution_convert_fusion.2
  47.9 1.3 fusion.108
  49.2 1.1 fusion.6
  50.4 1.5 copy-done.2
  51.9 1.2 fusion.75
  53.2 2.7 convolution_convert_fusion.1
  56.0 38.0 %reduce-scatter.5.cloned.1.call-done = bf16[2,256,768]{2,1,0:T(8,128)(2,1)} async-done(((bf16[8,256,768]{2,1,0:T(8,128)(2,1)}), bf16[2,256,768]{2,1,0:T(8,128)(2,1)}) %reduce-scatter.5.cloned.1.call-update) | async-done | bytes 786448 | tf_op jit(solution)/shard_map/reduce_scatter | solution.py:94
  93.9 1.5 fusion.77
  95.4 1.5 multiply_reduce_fusion.1
  97.0 1.3 add_convert_fusion.4
  98.6 11.4 %psum.63 = s32[2]{0:T(128)S(1)} all-reduce(s32[2]{0:T(128)S(1)} %select_reduce_fusion), channel_id=1, replica_groups=mesh['dp'=8,'mp'=4] {'dp'}, use_global_device_ids=true, to_apply=%region_10.11 | all-reduce | flops 2 | bytes 16 | tf_op jit(solution)/shard_map/psum | solution.py:55
  111.3 1.1 fusion.58
  112.5 1.7 collective-permute-start.2
  114.2 27.9 %collective-permute-done = bf16[2,256,768]{2,1,0:T(8,128)(2,1)} collective-permute-done((bf16[2,256,768]{2,1,0:T(8,128)(2,1)}, bf16[2,256,768]{2,1,0:T(8,128)(2,1)}, u32[]{:S(2)}, u32[]{:S(2)}) %collective-permute-start) | collective-permute-done | bytes 786464 | tf_op jit(solution)/shard_map/ppermute | solution.py:145
  142.8 11.2 %collective-permute-done.1 = bf16[2,256,768]{2,1,0:T(8,128)(2,1)} collective-permute-done((bf16[2,256,768]{2,1,0:T(8,128)(2,1)}, bf16[2,256,768]{2,1,0:T(8,128)(2,1)}, u32[]{:S(2)}, u32[]{:S(2)}) %collective-permute-start.1) | collective-permute-done | bytes 786464 | tf_op jit(solution)/shard_map/ppermute | solution.py:145
  154.1 3.1 pad_maximum_fusion.2
  157.2 4.3 gather_fusion
  161.5 4.2 broadcast_multiply_fusion
  165.6 4.5 fusion.80
  170.2 5.1 fusion.24
  175.3 4.5 fusion.68
  179.8 14.7 %multiply_convert_fusion.1 = (bf16[8,256,768]{2,1,0:T(8,128)(2,1)}, f32[8,256,768]{2,1,0:T(8,128)S(1)}) fusion(f32[8,256,768]{2,1,0:T(8,128)S(1)} %get-tuple-element.45, u8[256,768]{1,0:T(8,128)(4,1)S(1)} %get-tuple-element.12, u8[256,768]{1,0:T(8,128)(4,1)S(1)} %get-tuple-element.11), kind=kLoop, calls=%fused_computation.14 | loop fusion | flops 110100480 | bytes 16121856 | tf_op jit(solution)/shard_map/convert_element_type | solution.py:113
  194.5 8.3 %add_convert_fusion.1 = bf16[8,256,768]{2,1,0:T(8,128)(2,1)} fusion(f32[8,256,768]{2,1,0:T(8,128)S(1)} %get-tuple-element.32, f32[8,256,768]{2,1,0:T(8,128)} %fusion.80, f32[8,256,768]{2,1,0:T(8,128)S(1)} %get-tuple-element.45, bf16[8,256,768]{2,1,0:T(8,128)(2,1)S(1)} %bitcast.148, bf16[2,768,768]{2,1,0:T(8,128)(2,1)} %param.21), kind=kOutput, calls=%fused_computation.12 | convolution fusion | flops 2439512064 | bytes 26345472 | tf_op jit(solution)/shard_map/rsd,fd->rsf/dot_general | solution.py:156
  202.8 5.1 fusion.13
  207.9 4.1 add_convert_fusion
  212.1 38.0 %reduce-scatter.9.cloned.1.call-done = bf16[2,256,768]{2,1,0:T(8,128)(2,1)} async-done(((bf16[8,256,768]{2,1,0:T(8,128)(2,1)}), bf16[2,256,768]{2,1,0:T(8,128)(2,1)}) %reduce-scatter.9.cloned.1.call-update) | async-done | bytes 786448 | tf_op jit(solution)/shard_map/reduce_scatter | solution.py:185
  250.1 1.9 convert_reduce_fusion.1
  251.9 2.2 fusion.56
  254.1 1.7 fusion.96
  256.1 28.4 %all-gather.8.cloned.1.call-done = bf16[8,256,768]{2,1,0:T(8,128)(2,1)} async-done(((bf16[2,256,768]{2,1,0:T(8,128)(2,1)}), bf16[8,256,768]{2,1,0:T(8,128)(2,1)}) %all-gather.8.cloned.1.call-update) | async-done | bytes 3145744 | tf_op jit(solution)/shard_map/all_gather | solution.py:191
  284.5 3.2 convolution_convert_fusion.3
  287.8 7.0 multiply_reduce_fusion
  294.9 4.5 multiply_convert_fusion
  300.0 1.1 multiply_bitcast_fusion
  301.0 1.1 fusion.72
  302.4 1.4 copy-done.6
  304.2 4.1 convolution_convert_fusion
  308.3 5.1 fusion.17
  313.4 4.1 add_convert_fusion.2
  317.8 2.6 bitcast_multiply_fusion.1
  320.8 2.8 convolution_bitcast_fusion
  323.5 2.7 convolution_bitcast_fusion.1
  326.3 2.7 pad_maximum_fusion.1
  329.0 0.7 copy-done.25
  329.7 1.1 copy-done.33
  330.8 2.8 fusion.45
  333.7 2.8 fusion.48
  336.6 2.7 pad_maximum_fusion
  340.3 1.6 convolution_bitcast_fusion.2
  342.2 3.5 fusion.69
  346.4 1.7 convert_reduce_fusion
  348.1 2.1 fusion.57
  350.2 40.3 %all-reduce = (f32[768]{0:T(1024)}, f32[768]{0:T(1024)}, f32[768]{0:T(1024)}, f32[768]{0:T(1024)}) all-reduce(f32[768]{0:T(1024)S(1)} %get-tuple-element.15, f32[768]{0:T(1024)S(1)} %get-tuple-element.19, f32[768]{0:T(1024)S(1)} %get-tuple-element.13, f32[768]{0:T(1024)S(1)} %get-tuple-element.17), channel_id=1, replica_groups=mesh['dp'=8,'mp'=4] {'dp','mp'}, use_global_device_ids=true, to_apply=%region_25.26 | all-reduce | flops 3072 | bytes 24576 | tf_op jit(solution)/shard_map/psum | solution.py:242
  390.5 3.7 add_add_fusion.2
  394.2 360.0 %all-reduce.4.cloned.1.call-done = (f32[768,3,192]{0,2,1:T(8,128)}, f32[192,768]{1,0:T(8,128)}, f32[2,768,768]{2,1,0:T(8,128)}, f32[2,768,768]{2,1,0:T(8,128)}) async-done(((f32[768,3,192]{0,2,1:T(8,128)}, f32[192,768]{1,0:T(8,128)}, f32[2,768,768]{2,1,0:T(8,128)}, f32[2,768,768]{2,1,0:T(8,128)}), (f32[768,3,192]{0,2,1:T(8,128)}, f32[192,768]{1,0:T(8,128)}, f32[2,768,768]{2,1,0:T(8,128)}, ...) | async-done | bytes 11796496 | tf_op jit(solution)/shard_map/psum | solution.py:245
  754.3 2.9 copy.95
  757.2 2.1 copy.96
  759.3 2.2 copy.97
  761.5 2.2 copy.98
  (123 shorter events, 6.9 us)
Async XLA Ops:
  7.2 36.8 %copy-start = (bf16[768,3,192]{0,2,1:T(8,128)(2,1)S(1)}, bf16[768,3,192]{0,2,1:T(8,128)(2,1)}, u32[]{:S(2)}) copy-start(bf16[768,3,192]{0,2,1:T(8,128)(2,1)} %param.18) | copy-start | bytes 2654212
  7.2 5.5 copy-start.20
  7.2 5.5 copy-start.21
  7.2 36.8 %all-gather.4.cloned.1.call-start = ((), (), s32[]{:S(2)}) async-start(), calls=%async_computation.4 | async-start | bytes 3932160 | tf_op jit(solution)/shard_map/all_gather | solution.py:59
  12.6 81.4 %reduce-scatter.5.cloned.1.call-start = ((), (), s32[]{:S(2)}) async-start(), calls=%async_computation.5 | async-start | bytes 3932160 | tf_op jit(solution)/shard_map/reduce_scatter | solution.py:94
  47.9 2.5 copy-start.15
  49.2 2.7 copy-start.2
  51.9 1.2 copy-start.17
  53.1 2.8 copy-start.11
  53.2 40.8 %copy-start.1 = (bf16[2,256,768]{2,1,0:T(8,128)(2,1)S(1)}, bf16[2,256,768]{2,1,0:T(8,128)(2,1)}, u32[]{:S(2)}) copy-start(bf16[2,256,768]{2,1,0:T(8,128)(2,1)} %param.13) | copy-start | bytes 2359300
  55.9 41.1 %copy-start.18 = (f32[768]{0:T(1024)S(1)}, f32[768]{0:T(1024)}, u32[]{:S(2)}) copy-start(f32[768]{0:T(1024)} %param.24) | copy-start | bytes 9220
  55.9 41.1 %copy-start.22 = (f32[768]{0:T(1024)S(1)}, f32[768]{0:T(1024)}, u32[]{:S(2)}) copy-start(f32[768]{0:T(1024)} %param.25) | copy-start | bytes 9220
  55.9 42.6 %copy-start.30 = (s32[8]{0:T(128)S(1)}, s32[8]{0:T(128)}, u32[]{:S(2)}) copy-start(s32[8]{0:T(128)} %param.17) | copy-start | bytes 100
  55.9 55.4 %copy-start.4 = (bf16[2,256,768]{2,1,0:T(8,128)(2,1)S(1)}, bf16[2,256,768]{2,1,0:T(8,128)(2,1)}, u32[]{:S(2)}) copy-start(bf16[2,256,768]{2,1,0:T(8,128)(2,1)} %param.14) | copy-start | bytes 2359300
  55.9 114.3 %all-gather.6.cloned.1.call-start = ((), (), s32[]{:S(2)}) async-start(), calls=%async_computation.6 | async-start | bytes 3932160 | tf_op jit(solution)/shard_map/all_gather | solution.py:104
  93.9 3.1 copy-start.3
  98.3 151.7 %reduce-scatter.9.cloned.1.call-start = ((), (), s32[]{:S(2)}) async-start(), calls=%async_computation.8 | async-start | bytes 3932160 | tf_op jit(solution)/shard_map/reduce_scatter | solution.py:185
  110.0 47.2 %copy-start.31 = (s32[2]{0:T(128)}, s32[2]{0:T(128)S(1)}, u32[]{:S(2)}) copy-start(s32[2]{0:T(128)S(1)} %psum.63) | copy-start | bytes 28
  112.5 29.7 %collective-permute-start = (bf16[2,256,768]{2,1,0:T(8,128)(2,1)}, bf16[2,256,768]{2,1,0:T(8,128)(2,1)}, u32[]{:S(2)}, u32[]{:S(2)}) collective-permute-start(bf16[2,256,768]{2,1,0:T(8,128)(2,1)} %fusion.58), channel_id=1, source_target_pairs={{0,1},{1,2},{2,3},{3,0},{4,5},{5,6},{6,7},{7,4},{8,9},{9,10},{10,1... | collective-permute-start | bytes 2359304 | tf_op jit(solution)/shard_map/ppermute | solution.py:145
  112.5 30.4 %collective-permute-start.2 = (bf16[2,256,768]{2,1,0:T(8,128)(2,1)}, bf16[2,256,768]{2,1,0:T(8,128)(2,1)}, u32[]{:S(2)}, u32[]{:S(2)}) collective-permute-start(bf16[2,256,768]{2,1,0:T(8,128)(2,1)} %fusion.58), channel_id=1, source_target_pairs={{1,0},{2,1},{3,2},{0,3},{5,4},{6,5},{7,6},{4,7},{9,8},{10,9},{11,1... | collective-permute-start | bytes 2359304 | tf_op jit(solution)/shard_map/ppermute | solution.py:147
  142.1 11.9 %collective-permute-start.1 = (bf16[2,256,768]{2,1,0:T(8,128)(2,1)}, bf16[2,256,768]{2,1,0:T(8,128)(2,1)}, u32[]{:S(2)}, u32[]{:S(2)}) collective-permute-start(bf16[2,256,768]{2,1,0:T(8,128)(2,1)} %collective-permute-done), channel_id=1, source_target_pairs={{0,1},{1,2},{2,3},{3,0},{4,5},{5,6},{6,7},{7,4},{8,9},{9,10},{10,1... | collective-permute-start | bytes 2359304 | tf_op jit(solution)/shard_map/ppermute | solution.py:145
  161.5 4.2 copy-start.28
  170.2 5.1 copy-start.24
  170.2 5.1 copy-start.26
  179.8 14.7 %copy-start.9 = (bf16[4,2,256,768]{3,2,1,0:T(8,128)(2,1)S(1)}, bf16[4,2,256,768]{3,2,1,0:T(8,128)(2,1)}, u32[]{:S(2)}) copy-start(bf16[4,2,256,768]{3,2,1,0:T(8,128)(2,1)} %get-tuple-element.35) | copy-start | bytes 9437188
  202.8 5.1 copy-start.27
  202.8 5.1 copy-start.32
  212.0 72.5 %all-gather.8.cloned.1.call-start = ((), (), s32[]{:S(2)}) async-start(), calls=%async_computation.9 | async-start | bytes 3932160 | tf_op jit(solution)/shard_map/all_gather | solution.py:191
  250.1 4.1 copy-start.5
  255.9 90.4 %reduce-scatter.11.cloned.1.call-start = ((), (), s32[]{:S(2)}) async-start(), calls=%async_computation.10 | async-start | bytes 3932160 | tf_op jit(solution)/shard_map/reduce_scatter | solution.py:231
  284.5 3.2 copy-start.16
  287.8 7.1 slice-start
  287.8 7.1 slice-start.1
  302.4 1.4 copy-start.6
  308.2 82.3 %reduce-scatter.7.cloned.1.call-start = ((), (), s32[]{:S(2)}) async-start(), calls=%async_computation.7 | async-start | bytes 3932160 | tf_op jit(solution)/shard_map/reduce_scatter | solution.py:124
  308.3 5.1 copy-start.13
  308.3 5.1 copy-start.29
  317.5 436.7 %all-reduce.4.cloned.1.call-start = ((), (), s32[]{:S(2)}) async-start(), calls=%async_computation.11 | async-start | bytes 23592960 | tf_op jit(solution)/shard_map/psum | solution.py:245
  317.8 3.0 copy-start.14
  326.3 3.5 copy-start.25
  326.3 4.6 copy-start.33
  336.5 3.4 copy-start.10
  336.5 3.8 copy-start.12
  336.6 5.4 copy-start.23
  340.3 1.9 copy-start.7
  345.7 0.7 copy-start.19
  754.3 5.0 copy-start.8
  757.2 4.3 slice-start.2
  759.3 2.2 slice-start.3
Sparse Core Ops, SparseCore 0:
  12.7 31.2 all-gather.3
  56.0 37.8 reduce-scatter.4
  98.5 38.2 all-gather.5
  212.2 37.8 reduce-scatter.8
  256.0 28.4 all-gather.7
  308.4 37.8 reduce-scatter.10
  348.8 38.0 reduce-scatter.6
  392.1 362.1 all-reduce.3
